TPU v7x, 512 devices: a whole 4x8x8 slice. The times are simulated.
512 devices in a mesh: seq: 16 (over z, core), expert: 32 (over x, y).
Axes of the slice: x: 4, y: 8, z: 8, core: 2. Of those that a mesh axis runs over, the one named last changes fastest.
Arguments:
- hidden: bfloat16 [32, 1024, 2048], P('expert', 'seq'), may hold values from -6 to 6
- queries: bfloat16 [32, 1024, 4608], P('expert', 'seq'), may hold values from -5 to 5
- suffix_latent: bfloat16 [32, 1024, 576], P('expert', 'seq'), may hold values from -6 to 6
- prefix_latent: bfloat16 [2, 1024, 576], P(None, 'seq'), may hold values from -6 to 6
- lengths: int32 [32, 4], P('expert'), may hold values from 1 to 512, 1024 in all within a row
- prefix_of: int32 [32, 4], P('expert'), may hold values from 0 to 1
- value_up: bfloat16 [8, 512, 128], replicated, may hold values from -1 to 1
- out_proj: bfloat16 [1024, 2048], P(None, 'expert'), may hold values from -0.1875 to 0.1875
- norm_gain: float32 [2048], replicated, may hold values from 0.5 to 1.5
- router: bfloat16 [2048, 32], replicated, may hold values from -0.0625 to 0.0625
- routes: int32 [32, 1024, 6], P('expert', 'seq'), may hold values from 0 to 31, all different within a row; in each aligned block of 64 rows (0 to 63, 64 to 127, ..., all dimensions but the last counted through in order) at most 16 rows name the same one
- expert_in: bfloat16 [32, 2048, 1408], P('expert', 'seq'), may hold values from -0.125 to 0.125
- expert_out: bfloat16 [32, 2048, 704], P('expert', 'seq'), may hold values from -1.25 to 1.25
Outputs:
- layer_out: bfloat16 [32, 1024, 2048], P('expert', 'seq')
Inputs may be any that keep to these rules, and one draw needn't show every extreme that they name: `routes`: among the rows of one device (aligned blocks of 64 tokens) no expert is named more than 16 times, a bound that some block reaches; a token's 6 experts differ. `lengths`: each row sums to 1024; its longest request has exactly 512 tokens.
All inputs are finite; a program needn't handle non-finite values.
Results may differ from a plain program's by a relative error of at most 0.013.
Values may be sent and summed in bfloat16 or wider, within the bound.
No kernel may reach another device: no remote copies, remote signals or barrier semaphores. Data moves between devices by JAX's collectives and lax.ppermute only.
A program may use at most 128 MiB of HBM per device.

v0:
```python
import jax
import jax.numpy as jnp
from jax import lax
from jax.sharding import PartitionSpec as P

qk_scale = 192.0 ** (-0.5)
big_negative = -1e30


def request_of(positions, request_ends):
    return jnp.sum((positions[:, None] >= request_ends[None, :]).astype(jnp.int32), axis=1)


def merge_scores(running, scores, allowed, values):
    running_max, running_sum, running_acc = running
    new_max = jnp.maximum(running_max, jnp.max(jnp.where(allowed, scores, big_negative), axis=2))
    weights = jnp.where(allowed, jnp.exp(scores - new_max[:, :, None]), 0.0)
    new_sum = jnp.sum(weights, axis=2)
    new_acc = jnp.einsum(
        "thn,nl->thl", weights.astype(jnp.bfloat16), values, preferred_element_type=jnp.float32
    )
    return (new_max, new_sum, new_acc)


def local(
    hidden,
    queries,
    suffix_latent,
    prefix_latent,
    lengths,
    prefix_of,
    value_up,
    out_proj,
    norm_gain,
    router,
    routes,
    expert_in,
    expert_out,
):
    local_tokens = hidden.shape[1]
    model_width = hidden.shape[2]
    key_width = suffix_latent.shape[2]
    head_count = value_up.shape[0]
    latent_width = value_up.shape[1]
    expert_count = router.shape[1]
    top_count = routes.shape[2]
    capacity = 4 * local_tokens * top_count // (3 * expert_count)
    request_count = lengths.shape[1]
    request_ends = jnp.cumsum(lengths[0])
    my_positions = lax.axis_index("seq") * local_tokens + jnp.arange(local_tokens, dtype=jnp.int32)
    my_requests = request_of(my_positions, request_ends)
    request_ids = jnp.arange(request_count, dtype=jnp.int32)
    chosen = jnp.sum(
        jnp.where(my_requests[:, None] == request_ids[None, :], prefix_of[0][None, :], 0), axis=1
    )
    prefix_pick = chosen[:, None] == jnp.arange(2, dtype=jnp.int32)[None, :]
    single_prefix = jnp.all(chosen == chosen[0])
    my_prefix = chosen[0]
    query_rows = queries[0].reshape(local_tokens, head_count, key_width)
    start_state = (
        jnp.full((local_tokens, head_count), big_negative, jnp.float32),
        jnp.zeros((local_tokens, head_count), jnp.float32),
        jnp.zeros((local_tokens, head_count, latent_width), jnp.float32),
    )
    suffix_piece = lax.all_gather(suffix_latent, "seq", axis=1, tiled=True)
    prefix_piece = lax.all_gather(prefix_latent, "seq", axis=1, tiled=True)
    piece_rows = suffix_piece.shape[1]
    suffix_keys = suffix_piece[0]
    key_positions = jnp.arange(piece_rows, dtype=jnp.int32)
    key_requests = request_of(key_positions, request_ends)
    suffix_allowed = (key_requests[None, :] == my_requests[:, None]) & (
        key_positions[None, :] <= my_positions[:, None]
    )
    suffix_scores = (
        jnp.einsum("thk,nk->thn", query_rows, suffix_keys, preferred_element_type=jnp.float32)
        * qk_scale
    )

    def one_prefix(running_state):
        chosen_keys = lax.dynamic_index_in_dim(prefix_piece, my_prefix, 0, keepdims=False)
        prefix_scores = (
            jnp.einsum("thk,nk->thn", query_rows, chosen_keys, preferred_element_type=jnp.float32)
            * qk_scale
        )
        scores = jnp.concatenate([suffix_scores, prefix_scores], axis=2)
        every_key = jnp.ones((local_tokens, piece_rows), dtype=bool)
        allowed = jnp.concatenate([suffix_allowed, every_key], axis=1)[:, None, :]
        values = jnp.concatenate(
            [suffix_keys[:, :latent_width], chosen_keys[:, :latent_width]], axis=0
        )
        return merge_scores(running_state, scores, allowed, values)

    def two_prefixes(running_state):
        prefix_scores = (
            jnp.einsum(
                "thk,pnk->thpn", query_rows, prefix_piece, preferred_element_type=jnp.float32
            )
            * qk_scale
        )
        scores = jnp.concatenate(
            [suffix_scores, prefix_scores.reshape(local_tokens, head_count, 2 * piece_rows)], axis=2
        )
        prefix_allowed = jnp.broadcast_to(
            prefix_pick[:, :, None], (local_tokens, 2, piece_rows)
        ).reshape(local_tokens, 2 * piece_rows)
        allowed = jnp.concatenate([suffix_allowed, prefix_allowed], axis=1)[:, None, :]
        values = jnp.concatenate(
            [
                suffix_keys[:, :latent_width],
                prefix_piece[:, :, :latent_width].reshape(2 * piece_rows, latent_width),
            ],
            axis=0,
        )
        return merge_scores(running_state, scores, allowed, values)

    final_max, final_sum, final_acc = lax.cond(single_prefix, one_prefix, two_prefixes, start_state)
    latent_out = (final_acc / final_sum[:, :, None]).astype(jnp.bfloat16)
    value_out = jnp.einsum(
        "thl,hlv->thv", latent_out, value_up, preferred_element_type=jnp.float32
    ).astype(jnp.bfloat16)
    value_out = value_out.reshape(local_tokens, head_count * value_up.shape[2])
    projected = jnp.dot(
        value_out,
        lax.all_gather(out_proj, "expert", axis=1, tiled=True),
        preferred_element_type=jnp.float32,
    )
    residual = hidden[0].astype(jnp.float32) + projected
    normed = (
        residual
        * lax.rsqrt(jnp.mean(residual * residual, axis=1, keepdims=True) + 1e-06)
        * norm_gain
    ).astype(jnp.bfloat16)
    logits = jnp.dot(normed, router, preferred_element_type=jnp.float32)
    expert_probs = jax.nn.softmax(logits, axis=1)
    expert_ids = jnp.arange(expert_count, dtype=jnp.int32)
    my_routes = routes[0]
    matches = my_routes[:, :, None] == expert_ids[None, None, :]
    gate_values = jnp.sum(jnp.where(matches, expert_probs[:, None, :], 0.0), axis=2)
    flat_hits = matches.reshape(local_tokens * top_count, expert_count).astype(jnp.int32)
    earlier = jnp.cumsum(flat_hits, axis=0) - flat_hits
    slot_index = jnp.sum(earlier * flat_hits, axis=1).reshape(local_tokens, top_count)
    cell_index = my_routes * capacity + slot_index
    cell_ids = jnp.arange(expert_count * capacity, dtype=jnp.int32)
    placing = jnp.sum(
        (cell_ids[:, None, None] == cell_index[None, :, :]).astype(jnp.int32), axis=2
    ).astype(jnp.bfloat16)
    outgoing = jnp.dot(placing, normed, preferred_element_type=jnp.float32).astype(jnp.bfloat16)
    outgoing = outgoing.reshape(expert_count, capacity, model_width)
    incoming = lax.all_to_all(outgoing, "expert", split_axis=0, concat_axis=0, tiled=True)
    full_in, full_out = (
        lax.all_gather(expert_in, "seq", axis=1, tiled=True),
        lax.all_gather(expert_out, "seq", axis=1, tiled=True),
    )
    all_rows = incoming.reshape(-1, model_width)
    gate_up = jnp.dot(all_rows, full_in[0], preferred_element_type=jnp.float32)
    hidden_units = gate_up.shape[1] // 2
    active = (jax.nn.silu(gate_up[:, :hidden_units]) * gate_up[:, hidden_units:]).astype(
        jnp.bfloat16
    )
    produced = lax.dot_general(
        active, full_out[0], (((1,), (1,)), ((), ())), preferred_element_type=jnp.float32
    ).astype(jnp.bfloat16)
    returned = lax.all_to_all(
        produced.reshape(-1, capacity, model_width),
        "expert",
        split_axis=0,
        concat_axis=0,
        tiled=True,
    )
    returned_rows = returned.reshape(-1, model_width)
    picked = returned_rows[cell_index]
    routed_sum = jnp.sum(gate_values[:, :, None] * picked.astype(jnp.float32), axis=1)
    layer_out = (residual + routed_sum).astype(jnp.bfloat16)
    return layer_out[None]


def solution(mesh):
    in_specs = (
        P("expert", "seq", None),
        P("expert", "seq", None),
        P("expert", "seq", None),
        P(None, "seq", None),
        P("expert", None),
        P("expert", None),
        P(),
        P(None, "expert"),
        P(),
        P(),
        P("expert", "seq", None),
        P("expert", "seq", None),
        P("expert", "seq", None),
    )
    out_specs = P("expert", "seq", None)
    return jax.shard_map(local, mesh=mesh, in_specs=in_specs, out_specs=out_specs, check_vma=False)
```

profile of v0, /device:TPU:16, one launch (start us, length us, event | category | flops | bytes accessed | tf_op | source)
XLA Modules:
  0.0 368.0 jit_solution(16596417180253832410)
XLA Ops:
  13.9 2.4 reshape_squeeze.3
  20.0 36.3 %all-gather.8.cloned.1.call-done = bf16[1,1024,576]{2,1,0:T(8,128)(2,1)} async-done(((bf16[1,64,576]{2,1,0:T(8,128)(2,1)}), bf16[1,1024,576]{2,1,0:T(8,128)(2,1)}) %all-gather.8.cloned.1.call-update) | async-done | bytes 1179664 | tf_op jit(solution)/shard_map/all_gather | solution.py:65
  56.3 2.4 copy.87
  58.7 2.5 convolution_multiply_fusion
  61.3 39.0 %all-gather.6.cloned.1.call-done = bf16[2,1024,576]{2,0,1:T(2,128)(2,1)} async-done(((bf16[2,64,576]{2,0,1:T(2,128)(2,1)}), bf16[2,1024,576]{2,0,1:T(2,128)(2,1)}) %all-gather.6.cloned.1.call-update) | async-done | bytes 2359312 | tf_op jit(solution)/shard_map/all_gather | solution.py:66
  100.3 31.3 %conditional.1 = (f32[64,8,512]{2,1,0:T(8,128)}, f32[64,8]{1,0:T(8,128)S(1)}) conditional(s32[]{:T(128)} %convert_element_type.64, (s32[64]{0:T(128)S(1)}, s32[64,2]{1,0:T(8,128)S(1)}, pred[64,1024]{1,0:T(8,128)(4,1)S(1)}, bf16[64,8,576]{2,1,0:T(8,128)(2,1)}, bf16[2,1024,576]{2,0,1:T(2,128)(2,1)}, /*index=5*/f32[64,8,1024]{2,1,0:T(8,128)S(1)}, ...), branch_computations={%region_5.8_spmd, %region_8.11_spmd} | conditional | flops 2843409920 | bytes 92157032 | solution.py:116
  100.3 7.4 %copy.88 = bf16[2,1024,576]{1,2,0:T(8,128)(2,1)} copy(bf16[2,1024,576]{2,0,1:T(2,128)(2,1)} %get-tuple-element.110) | data formatting | bytes 4718592 | tf_op jit(solution)/shard_map
  107.6 3.7 fusion.10
  116.0 4.0 %copy.82 = bf16[2,1024,512]{2,1,0:T(8,128)(2,1)} copy(bf16[2,1024,512]{1,2,0:T(8,128)(2,1)} %slice.36) | data formatting | bytes 4194304 | tf_op jit(solution)/shard_map/cond/branch_0_fun/slice | solution.py:110
  120.0 2.4 copy.89
  123.7 5.9 %fusion.2 = f32[64,8,512]{2,1,0:T(8,128)} fusion(bf16[2048,512]{1,0:T(8,128)(2,1)} %bitcast.104, bf16[1024,512]{1,0:T(8,128)(2,1)S(1)} %slice.35, f32[64,8,2048]{2,1,0:T(8,128)} %bitcast.98, f32[64,8,1024]{2,1,0:T(8,128)S(1)} %get-tuple-element.36, f32[64,8]{1,0:T(8,128)S(1)} %broadcast_maximum_fusion, pred[64,3072]{1,0:T(8,128)(4,1)S(1)} %pad_add_fusion), kind=kOutput, calls=%fused_computation.7 | convolution fusion | flops 1623195648 | bytes 10684416 | tf_op jit(solution)/shard_map/cond/branch_0_fun/thn,nl->thl/dot_general | solution.py:19
  133.4 54.2 %all-gather.10.cloned.1.call-done = bf16[1024,2048]{0,1:T(8,128)(2,1)} async-done(((bf16[1024,64]{0,1:T(8,128)(2,1)}), bf16[1024,2048]{0,1:T(8,128)(2,1)}) %all-gather.10.cloned.1.call-update) | async-done | bytes 4194320 | tf_op jit(solution)/shard_map/all_gather | solution.py:124
  187.6 3.7 %multiply_reduce_fusion.1 = (f32[64]{0:T(128)S(1)}, f32[64,2048]{1,0:T(8,128)S(1)}) fusion(bf16[1024,2048]{0,1:T(8,128)(2,1)} %all-gather.10.cloned.1.call-done, bf16[8,8,8,128]{3,2,1,0:T(8,128)(2,1)S(1)} %fusion.33, bf16[1,64,2048]{2,1,0:T(8,128)(2,1)S(1)} %copy-done.9), kind=kOutput, calls=%fused_computation.60 | convolution fusion | flops 268959680 | bytes 5112064 | tf_op jit(solution)/shard_map/dot_general | solution.py:122
  194.1 7.2 %all-to-all-start = ((bf16[32,16,2048]{2,1,0:T(8,128)(2,1)}), bf16[32,16,2048]{2,1,0:T(8,128)(2,1)S(1)}, u32[]{:S(2)}, u32[]{:S(2)}) async-start(bf16[32,16,2048]{2,1,0:T(8,128)(2,1)} %bitcast.20), calls=%async_computation | async-start | bytes 4194304 | tf_op jit(solution)/shard_map/all_to_all | solution.py:149
  201.3 34.9 %all-gather.12.cloned.1.call-done = bf16[1,2048,1408]{2,1,0:T(8,128)(2,1)} async-done(((bf16[1,128,1408]{2,1,0:T(8,128)(2,1)}), bf16[1,2048,1408]{2,1,0:T(8,128)(2,1)}) %all-gather.12.cloned.1.call-update) | async-done | bytes 5767184 | tf_op jit(solution)/shard_map/all_gather | solution.py:151
  236.2 11.3 %all-to-all-done = bf16[32,16,2048]{2,1,0:T(8,128)(2,1)S(1)} async-done(((bf16[32,16,2048]{2,1,0:T(8,128)(2,1)}), bf16[32,16,2048]{2,1,0:T(8,128)(2,1)S(1)}, u32[]{:S(2)}, u32[]{:S(2)}) %all-to-all-start) | async-done | bytes 2097184 | tf_op jit(solution)/shard_map/all_to_all | solution.py:149
  247.5 7.6 %fusion.28 = f32[512,1408]{1,0:T(8,128)} fusion(bf16[512,2048]{1,0:T(8,128)(2,1)S(1)} %bitcast.103, bf16[1,2048,1408]{2,1,0:T(8,128)(2,1)} %all-gather.12.cloned.1.call-done), kind=kOutput, calls=%fused_computation.40 | convolution fusion | flops 2952790016 | bytes 10747904 | tf_op jit(solution)/shard_map/dot_general | solution.py:155
  255.2 28.3 %all-gather.14.cloned.1.call-done = bf16[1,2048,704]{1,2,0:T(8,128)(2,1)} async-done(((bf16[1,128,704]{1,2,0:T(8,128)(2,1)}), bf16[1,2048,704]{1,2,0:T(8,128)(2,1)}) %all-gather.14.cloned.1.call-update) | async-done | bytes 2883600 | tf_op jit(solution)/shard_map/all_gather | solution.py:152
  283.5 6.0 %convolution_convert_fusion = bf16[512,2048]{1,0:T(8,128)(2,1)} fusion(bf16[1,2048,704]{1,2,0:T(8,128)(2,1)} %all-gather.14.cloned.1.call-done, f32[512,1408]{1,0:T(8,128)} %fusion.28), kind=kOutput, calls=%fused_computation.43 | convolution fusion | flops 1479606272 | bytes 8126464 | tf_op jit(solution)/shard_map/dot_general | solution.py:160
  289.5 10.0 %all-to-all-start.1 = ((bf16[32,16,2048]{2,1,0:T(8,128)(2,1)}), bf16[32,16,2048]{2,1,0:T(8,128)(2,1)S(1)}, u32[]{:S(2)}, u32[]{:S(2)}) async-start(bf16[32,16,2048]{2,1,0:T(8,128)(2,1)} %bitcast.102), calls=%async_computation.1 | async-start | bytes 4194304 | tf_op jit(solution)/shard_map/all_to_all | solution.py:163
  301.3 48.6 %all-to-all-done.1 = bf16[32,16,2048]{2,1,0:T(8,128)(2,1)S(1)} async-done(((bf16[32,16,2048]{2,1,0:T(8,128)(2,1)}), bf16[32,16,2048]{2,1,0:T(8,128)(2,1)S(1)}, u32[]{:S(2)}, u32[]{:S(2)}) %all-to-all-start.1) | async-done | bytes 2097184 | tf_op jit(solution)/shard_map/all_to_all | solution.py:163
  349.9 3.1 gather_fusion
  353.0 3.9 %reshape.155 = f32[64,6,2048]{2,1,0:T(8,128)} reshape(bf16[384,2048]{1,0:T(8,128)(2,1)} %gather_fusion) | data formatting | bytes 4718592 | tf_op jit(solution)/shard_map/convert_element_type | solution.py:172
  356.9 3.8 %multiply_reduce_fusion = f32[64,2048]{1,0:T(8,128)S(1)} fusion(f32[64,6,2048]{2,1,0:T(8,128)} %reshape.155, f32[64,6]{1,0:T(8,128)S(1)} %copy.96), kind=kLoop, calls=%fused_computation.42 | loop fusion | flops 1441792 | bytes 3671552 | tf_op jit(solution)/shard_map/reduce_sum | solution.py:172
  (77 shorter events, 25.3 us)
Async XLA Ops:
  6.5 126.4 %copy-start = (bf16[8,512,128]{2,1,0:T(8,128)(2,1)S(1)}, bf16[8,512,128]{2,1,0:T(8,128)(2,1)}, u32[]{:S(2)}) copy-start(bf16[8,512,128]{2,1,0:T(8,128)(2,1)} %param.21) | copy-start | bytes 3145732
  6.5 49.8 %all-gather.8.cloned.1.call-start = ((), (), s32[]{:S(2)}) async-start(), calls=%async_computation.3 | async-start | bytes 1392640 | tf_op jit(solution)/shard_map/all_gather | solution.py:65
  7.3 93.0 %all-gather.6.cloned.1.call-start = ((), (), s32[]{:S(2)}) async-start(), calls=%async_computation.2 | async-start | bytes 2785280 | tf_op jit(solution)/shard_map/all_gather | solution.py:66
  9.1 178.5 %all-gather.10.cloned.1.call-start = ((), (), s32[]{:S(2)}) async-start(), calls=%async_computation.4 | async-start | bytes 4325376 | tf_op jit(solution)/shard_map/all_gather | solution.py:124
  9.8 226.4 %all-gather.12.cloned.1.call-start = ((), (), s32[]{:S(2)}) async-start(), calls=%async_computation.5 | async-start | bytes 6127616 | tf_op jit(solution)/shard_map/all_gather | solution.py:151
  10.4 273.1 %all-gather.14.cloned.1.call-start = ((), (), s32[]{:S(2)}) async-start(), calls=%async_computation.6 | async-start | bytes 3063808 | tf_op jit(solution)/shard_map/all_gather | solution.py:152
  111.3 2.1 copy-start.1
  111.7 2.7 copy-start.4
  123.7 5.9 %copy-start.2 = (f32[64,8,2,1024]{3,1,2,0:T(8,128)S(1)}, f32[64,8,2,1024]{3,1,2,0:T(8,128)}, u32[]{:S(2)}) copy-start(f32[64,8,2,1024]{3,1,2,0:T(8,128)} %copy-done.1) | copy-start | bytes 12582916 | tf_op jit(solution)/shard_map/cond
  131.5 56.0 %copy-start.9 = (bf16[1,64,2048]{2,1,0:T(8,128)(2,1)S(1)}, bf16[1,64,2048]{2,1,0:T(8,128)(2,1)}, u32[]{:S(2)}) copy-start(bf16[1,64,2048]{2,1,0:T(8,128)(2,1)} %param.15) | copy-start | bytes 786436
  133.3 58.7 %copy-start.8 = (s32[512,64]{0,1:T(8,128)S(1)}, s32[512,64]{0,1:T(8,128)}, u32[]{:S(2)}) copy-start(s32[512,64]{0,1:T(8,128)} %convert_reduce_fusion) | copy-start | bytes 393220
  133.3 58.7 %copy-start.11 = (f32[2048]{0:T(1024)S(1)}, f32[2048]{0:T(1024)}, u32[]{:S(2)}) copy-start(f32[2048]{0:T(1024)} %param.23) | copy-start | bytes 24580
  191.2 0.8 copy-start.5
  194.1 53.4 %all-to-all-start = ((bf16[32,16,2048]{2,1,0:T(8,128)(2,1)}), bf16[32,16,2048]{2,1,0:T(8,128)(2,1)S(1)}, u32[]{:S(2)}, u32[]{:S(2)}) async-start(bf16[32,16,2048]{2,1,0:T(8,128)(2,1)} %bitcast.20), calls=%async_computation | async-start | bytes 4194304 | tf_op jit(solution)/shard_map/all_to_all | solution.py:149
  289.5 10.0 %copy-start.12 = (s32[1,64,6]{1,0,2:T(1,128)S(1)}, s32[1,64,6]{1,0,2:T(1,128)}, u32[]{:S(2)}) copy-start(s32[1,64,6]{1,0,2:T(1,128)} %param.25) | copy-start | bytes 4612
  289.5 10.3 %copy-start.10 = (bf16[2048,32]{0,1:T(8,128)(2,1)S(1)}, bf16[2048,32]{0,1:T(8,128)(2,1)}, u32[]{:S(2)}) copy-start(bf16[2048,32]{0,1:T(8,128)(2,1)} %param.24) | copy-start | bytes 393220
  289.5 60.4 %all-to-all-start.1 = ((bf16[32,16,2048]{2,1,0:T(8,128)(2,1)}), bf16[32,16,2048]{2,1,0:T(8,128)(2,1)S(1)}, u32[]{:S(2)}, u32[]{:S(2)}) async-start(bf16[32,16,2048]{2,1,0:T(8,128)(2,1)} %bitcast.102), calls=%async_computation.1 | async-start | bytes 4194304 | tf_op jit(solution)/shard_map/all_to_all | solution.py:163
  356.9 3.8 %copy-start.6 = (f32[64,2048]{1,0:T(8,128)S(1)}, f32[64,2048]{1,0:T(8,128)}, u32[]{:S(2)}) copy-start(f32[64,2048]{1,0:T(8,128)} %copy-done.5) | copy-start | bytes 1572868
Sparse Core Ops, SparseCore 0:
  9.5 46.7 all-gather.7
  58.4 41.7 all-gather.5
  103.4 84.0 all-gather.9
  189.5 46.6 all-gather.11
  238.1 45.3 all-gather.13
where the time goes:
time: 369 us; the launch traced here: 368 us
  waiting for transfers between devices  255 us (69%)
  local copies, waits for them, and re-layouts  34.7 us (9%)
  matrix products  33.2 us (9%)
  starting transfers between devices  17.3 us (5%)
  between operations  14 us (4%)
  other arithmetic  13.5 us (4%)
    all_gather x1, waiting for transfers between devices, local(): lax.all_gather(out_proj, 'expert', axis=1, tiled=True)  54.2 us
    all_to_all x1, waiting for transfers between devices, local(): lax.all_to_all(produced.reshape(-1, capacity, model_width), 'expert', spl...  48.6 us
    all_gather x1, waiting for transfers between devices, local(): prefix_piece = lax.all_gather(prefix_latent, 'seq', axis=1, tiled=True)  39 us
    all_gather x1, waiting for transfers between devices, local(): suffix_piece = lax.all_gather(suffix_latent, 'seq', axis=1, tiled=True)  36.3 us
    all_gather x1, waiting for transfers between devices, local(): lax.all_gather(expert_in, 'seq', axis=1, tiled=True)  34.9 us
    all_gather x1, waiting for transfers between devices, local(): lax.all_gather(expert_out, 'seq', axis=1, tiled=True)  28.3 us
    all_to_all x1, waiting for transfers between devices, local(): lax.all_to_all(outgoing, 'expert', split_axis=0, concat_axis=0, tiled=True)  11.3 us
    all_to_all x1, starting transfers between devices, local(): lax.all_to_all(produced.reshape(-1, capacity, model_width), 'expert', spl...  9.96 us
  transfers between devices with their start and end apart: 7, of which 7 were waited for; matrix products, arithmetic and copies ran while one was open for 17% of the time, Pallas kernels for 0%

commit v1 on v0

--- a/solution.py
+++ b/solution.py
@@ -5,6 +5,20 @@
 
 qk_scale = 192.0 ** (-0.5)
 big_negative = -1e30
+
+
+def spots_write(packet):
+    nodes = lax.axis_size("seq")
+    vals = tuple(((to_i, (to_i + 1) % nodes) for to_i in range(nodes)))
+    block_now, new = ([packet], [packet])
+    parts_seen = tuple(((to_i, (to_i - 1) % nodes) for to_i in range(nodes)))
+    for _ in range(nodes // 2):
+        block_now.append(lax.ppermute(block_now[-1], "seq", vals))
+    for _ in range((nodes - 1) // 2):
+        piece_next = lax.ppermute(new[-1], "seq", parts_seen)
+        new.append(piece_next)
+    vec_out = jnp.concatenate([*block_now[::-1], *new[1:]], axis=1)
+    return jnp.roll(vec_out, (lax.axis_index("seq") - nodes // 2) * packet.shape[1], 1)
 
 
 def request_of(positions, request_ends):
@@ -149,7 +163,7 @@
     incoming = lax.all_to_all(outgoing, "expert", split_axis=0, concat_axis=0, tiled=True)
     full_in, full_out = (
         lax.all_gather(expert_in, "seq", axis=1, tiled=True),
-        lax.all_gather(expert_out, "seq", axis=1, tiled=True),
+        spots_write(expert_out),
     )
     all_rows = incoming.reshape(-1, model_width)
     gate_up = jnp.dot(all_rows, full_in[0], preferred_element_type=jnp.float32)

time: 369 us -> 342 us (0.927)
  the two profiles are of different devices: /device:TPU:16 before, /device:TPU:8 now
where the time goes in v1:
time: 342 us; the launch traced here: 341 us
  waiting for transfers between devices  180 us (53%)
  local copies, waits for them, and re-layouts  69.2 us (20%)
  starting transfers between devices  40.6 us (12%)
  matrix products  24.5 us (7%)
  between operations  14.2 us (4%)
  other arithmetic  12.6 us (4%)
    all_gather x1, waiting for transfers between devices, local(): lax.all_gather(out_proj, 'expert', axis=1, tiled=True)  69 us
    all_to_all x1, waiting for transfers between devices, local(): lax.all_to_all(produced.reshape(-1, capacity, model_width), 'expert', spl...  46.8 us
    unnamed x78, local copies, waits for them, and re-layouts  43.1 us
    all_gather x1, waiting for transfers between devices, local(): prefix_piece = lax.all_gather(prefix_latent, 'seq', axis=1, tiled=True)  37.3 us
    ppermute x7, starting transfers between devices, spots_write(): piece_next = lax.ppermute(new[-1], 'seq', parts_seen)  24.2 us
    ppermute x8, waiting for transfers between devices, spots_write(): block_now.append(lax.ppermute(block_now[-1], 'seq', vals))  19 us
    all_to_all x1, starting transfers between devices, local(): lax.all_to_all(produced.reshape(-1, capacity, model_width), 'expert', spl...  9.86 us
    another operation x2, local copies, waits for them, and re-layouts  8.56 us
  transfers between devices with their start and end apart: 21, of which 10 were waited for; matrix products, arithmetic and copies ran while one was open for 24% of the time, Pallas kernels for 0%

profile of v1, /device:TPU:8, one launch (start us, length us, event | category | flops | bytes accessed | tf_op | source)
XLA Modules:
  0.0 341.0 jit_solution(7662982555751663368)
XLA Ops:
  10.4 8.5 %collective-permute-start.8 = (bf16[1,128,704]{1,2,0:T(8,128)(2,1)}, bf16[1,128,704]{1,2,0:T(8,128)(2,1)S(1)}, u32[]{:S(2)}, u32[]{:S(2)}) collective-permute-start(bf16[1,128,704]{1,2,0:T(8,128)(2,1)} %param.27), channel_id=1, source_target_pairs={{0,480},{32,0},{64,32},{96,64},{128,96},{160,128},{192,160},{224,1... | collective-permute-start | bytes 540680 | tf_op jit(solution)/shard_map/ppermute | solution.py:18
  26.2 5.2 %collective-permute-done.1 = bf16[1,128,704]{1,2,0:T(8,128)(2,1)S(1)} collective-permute-done((bf16[1,128,704]{1,2,0:T(8,128)(2,1)S(1)}, bf16[1,128,704]{1,2,0:T(8,128)(2,1)S(1)}, u32[]{:S(2)}, u32[]{:S(2)}) %collective-permute-start.1) | collective-permute-done | bytes 180256 | tf_op jit(solution)/shard_map/ppermute | solution.py:16
  32.0 3.0 collective-permute-start.9
  34.9 3.5 %collective-permute-done.2 = bf16[1,128,704]{1,2,0:T(8,128)(2,1)S(1)} collective-permute-done((bf16[1,128,704]{1,2,0:T(8,128)(2,1)S(1)}, bf16[1,128,704]{1,2,0:T(8,128)(2,1)S(1)}, u32[]{:S(2)}, u32[]{:S(2)}) %collective-permute-start.2) | collective-permute-done | bytes 180256 | tf_op jit(solution)/shard_map/ppermute | solution.py:16
  38.5 3.4 collective-permute-start.10
  41.9 3.5 %collective-permute-done.3 = bf16[1,128,704]{1,2,0:T(8,128)(2,1)S(1)} collective-permute-done((bf16[1,128,704]{1,2,0:T(8,128)(2,1)S(1)}, bf16[1,128,704]{1,2,0:T(8,128)(2,1)S(1)}, u32[]{:S(2)}, u32[]{:S(2)}) %collective-permute-start.3) | collective-permute-done | bytes 180256 | tf_op jit(solution)/shard_map/ppermute | solution.py:16
  46.3 3.0 collective-permute-start.11
  49.3 3.0 collective-permute-done.4
  53.0 3.0 collective-permute-start.12
  63.5 37.3 %all-gather.5.cloned.1.call-done = bf16[2,1024,576]{2,0,1:T(2,128)(2,1)} async-done(((bf16[2,64,576]{2,0,1:T(2,128)(2,1)}), bf16[2,1024,576]{2,0,1:T(2,128)(2,1)}) %all-gather.5.cloned.1.call-update) | async-done | bytes 2359312 | tf_op jit(solution)/shard_map/all_gather | solution.py:80
  101.4 17.3 %conditional.1 = (f32[64,8,512]{2,1,0:T(8,128)}, f32[64,8]{1,0:T(8,128)S(1)}) conditional(s32[]{:T(128)} %convert_element_type.64, (s32[64]{0:T(128)S(1)}, s32[64,2]{1,0:T(8,128)}, pred[64,1024]{1,0:T(8,128)(4,1)}, bf16[64,8,576]{2,1,0:T(8,128)(2,1)}, bf16[2,1024,576]{2,0,1:T(2,128)(2,1)}, /*index=5*/f32[64,8,1024]{2,1,0:T(8,128)S(1)}, ...), branch_computations={%region_5.8_spmd, %region_8.11_spmd} | conditional | flops 2843409920 | bytes 58866812 | solution.py:130
  101.4 7.3 %copy.90 = bf16[2,1024,576]{1,2,0:T(8,128)(2,1)} copy(bf16[2,1024,576]{2,0,1:T(2,128)(2,1)} %get-tuple-element.115) | data formatting | bytes 4718592 | tf_op jit(solution)/shard_map
  120.5 69.0 %all-gather.9.cloned.1.call-done = bf16[1024,2048]{0,1:T(8,128)(2,1)} async-done(((bf16[1024,64]{0,1:T(8,128)(2,1)}), bf16[1024,2048]{0,1:T(8,128)(2,1)}) %all-gather.9.cloned.1.call-update) | async-done | bytes 4194320 | tf_op jit(solution)/shard_map/all_gather | solution.py:138
  189.4 3.7 %multiply_reduce_fusion.1 = (f32[64]{0:T(128)S(1)}, f32[64,2048]{1,0:T(8,128)S(1)}) fusion(bf16[1024,2048]{0,1:T(8,128)(2,1)} %all-gather.9.cloned.1.call-done, bf16[8,8,8,128]{3,2,1,0:T(8,128)(2,1)S(1)} %fusion.34, bf16[1,64,2048]{2,1,0:T(8,128)(2,1)} %param.15), kind=kOutput, calls=%fused_computation.61 | convolution fusion | flops 268959680 | bytes 5112064 | tf_op jit(solution)/shard_map/dot_general | solution.py:136
  196.2 5.9 %all-to-all-start = ((bf16[32,16,2048]{2,1,0:T(8,128)(2,1)}), bf16[32,16,2048]{2,1,0:T(8,128)(2,1)S(1)}, u32[]{:S(2)}, u32[]{:S(2)}) async-start(bf16[32,16,2048]{2,1,0:T(8,128)(2,1)} %bitcast.20), calls=%async_computation | async-start | bytes 4194304 | tf_op jit(solution)/shard_map/all_to_all | solution.py:163
  202.6 5.9 %collective-permute-done.13 = bf16[1,128,704]{1,2,0:T(8,128)(2,1)} collective-permute-done((bf16[1,128,704]{1,2,0:T(8,128)(2,1)}, bf16[1,128,704]{1,2,0:T(8,128)(2,1)}, u32[]{:S(2)}, u32[]{:S(2)}) %collective-permute-start.13) | collective-permute-done | bytes 180256 | tf_op jit(solution)/shard_map/ppermute | solution.py:18
  208.5 3.4 %collective-permute-start.14 = (bf16[1,128,704]{1,2,0:T(8,128)(2,1)}, bf16[1,128,704]{1,2,0:T(8,128)(2,1)S(1)}, u32[]{:S(2)}, u32[]{:S(2)}) collective-permute-start(bf16[1,128,704]{1,2,0:T(8,128)(2,1)} %collective-permute-done.13), channel_id=1, source_target_pairs={{0,480},{32,0},{64,32},{96,64},{128,96},{160,128},{192,160},{224,1... | collective-permute-start | bytes 540680 | tf_op jit(solution)/shard_map/ppermute | solution.py:18
  253.6 5.7 %fusion.28 = f32[512,1408]{1,0:T(8,128)S(1)} fusion(bf16[512,2048]{1,0:T(8,128)(2,1)S(1)} %bitcast.102, bf16[1,2048,1408]{2,1,0:T(8,128)(2,1)} %all-gather.11.cloned.1.call-done), kind=kOutput, calls=%fused_computation.40 | convolution fusion | flops 2952790016 | bytes 10747904 | tf_op jit(solution)/shard_map/dot_general | solution.py:169
  259.4 5.0 %convolution_convert_fusion = bf16[512,2048]{1,0:T(8,128)(2,1)} fusion(bf16[1,4096,704]{1,2,0:T(8,128)(2,1)} %constant_dynamic-update-slice_fusion, s32[]{:T(128)S(6)} %select_n.52, f32[512,1408]{1,0:T(8,128)S(1)} %fusion.28), kind=kOutput, calls=%fused_computation.43 | convolution fusion | flops 1479606272 | bytes 8126468 | tf_op jit(solution)/shard_map/dot_general | solution.py:174
  264.4 9.9 %all-to-all-start.1 = ((bf16[32,16,2048]{2,1,0:T(8,128)(2,1)}), bf16[32,16,2048]{2,1,0:T(8,128)(2,1)S(1)}, u32[]{:S(2)}, u32[]{:S(2)}) async-start(bf16[32,16,2048]{2,1,0:T(8,128)(2,1)} %bitcast.103), calls=%async_computation.1 | async-start | bytes 4194304 | tf_op jit(solution)/shard_map/all_to_all | solution.py:177
  276.1 46.8 %all-to-all-done.1 = bf16[32,16,2048]{2,1,0:T(8,128)(2,1)S(1)} async-done(((bf16[32,16,2048]{2,1,0:T(8,128)(2,1)}), bf16[32,16,2048]{2,1,0:T(8,128)(2,1)S(1)}, u32[]{:S(2)}, u32[]{:S(2)}) %all-to-all-start.1) | async-done | bytes 2097184 | tf_op jit(solution)/shard_map/all_to_all | solution.py:177
  322.9 3.1 gather_fusion
  326.0 3.9 %reshape.155 = f32[64,6,2048]{2,1,0:T(8,128)} reshape(bf16[384,2048]{1,0:T(8,128)(2,1)} %gather_fusion) | data formatting | bytes 4718592 | tf_op jit(solution)/shard_map/convert_element_type | solution.py:186
  330.0 3.7 %multiply_reduce_fusion = f32[64,2048]{1,0:T(8,128)S(1)} fusion(f32[64,6,2048]{2,1,0:T(8,128)} %reshape.155, f32[64,6]{1,0:T(8,128)S(1)} %copy.96), kind=kLoop, calls=%fused_computation.42 | loop fusion | flops 1441792 | bytes 3671552 | tf_op jit(solution)/shard_map/reduce_sum | solution.py:186
  (165 shorter events, 80.0 us)
Async XLA Ops:
  6.5 113.5 %copy-start = (bf16[8,512,128]{2,1,0:T(8,128)(2,1)S(1)}, bf16[8,512,128]{2,1,0:T(8,128)(2,1)}, u32[]{:S(2)}) copy-start(bf16[8,512,128]{2,1,0:T(8,128)(2,1)} %param.21) | copy-start | bytes 3145732
  6.5 52.0 %all-gather.7.cloned.1.call-start = ((), (), s32[]{:S(2)}) async-start(), calls=%async_computation.3 | async-start | bytes 1392640 | tf_op jit(solution)/shard_map/all_gather | solution.py:79
  7.3 93.5 %all-gather.5.cloned.1.call-start = ((), (), s32[]{:S(2)}) async-start(), calls=%async_computation.2 | async-start | bytes 2785280 | tf_op jit(solution)/shard_map/all_gather | solution.py:80
  9.1 180.3 %all-gather.9.cloned.1.call-start = ((), (), s32[]{:S(2)}) async-start(), calls=%async_computation.4 | async-start | bytes 4325376 | tf_op jit(solution)/shard_map/all_gather | solution.py:138
  9.8 243.8 %all-gather.11.cloned.1.call-start = ((), (), s32[]{:S(2)}) async-start(), calls=%async_computation.5 | async-start | bytes 6127616 | tf_op jit(solution)/shard_map/all_gather | solution.py:165
  10.4 14.9 %collective-permute-start = (bf16[1,128,704]{1,2,0:T(8,128)(2,1)}, bf16[1,128,704]{1,2,0:T(8,128)(2,1)S(1)}, u32[]{:S(2)}, u32[]{:S(2)}) collective-permute-start(bf16[1,128,704]{1,2,0:T(8,128)(2,1)} %param.27), channel_id=1, source_target_pairs={{0,32},{32,64},{64,96},{96,128},{128,160},{160,192},{192,224},{224... | collective-permute-start | bytes 540680 | tf_op jit(solution)/shard_map/ppermute | solution.py:16
  10.4 21.5 %collective-permute-start.8 = (bf16[1,128,704]{1,2,0:T(8,128)(2,1)}, bf16[1,128,704]{1,2,0:T(8,128)(2,1)S(1)}, u32[]{:S(2)}, u32[]{:S(2)}) collective-permute-start(bf16[1,128,704]{1,2,0:T(8,128)(2,1)} %param.27), channel_id=1, source_target_pairs={{0,480},{32,0},{64,32},{96,64},{128,96},{160,128},{192,160},{224,1... | collective-permute-start | bytes 540680 | tf_op jit(solution)/shard_map/ppermute | solution.py:18
  25.3 76.0 %copy-start.8 = (bf16[1,128,704]{1,2,0:T(8,128)(2,1)}, bf16[1,128,704]{1,2,0:T(8,128)(2,1)S(1)}, u32[]{:S(2)}) copy-start(bf16[1,128,704]{1,2,0:T(8,128)(2,1)S(1)} %collective-permute-done) | copy-start | bytes 540676
  25.3 6.1 %collective-permute-start.1 = (bf16[1,128,704]{1,2,0:T(8,128)(2,1)S(1)}, bf16[1,128,704]{1,2,0:T(8,128)(2,1)S(1)}, u32[]{:S(2)}, u32[]{:S(2)}) collective-permute-start(bf16[1,128,704]{1,2,0:T(8,128)(2,1)S(1)} %collective-permute-done), channel_id=1, source_target_pairs={{0,32},{32,64},{64,96},{96,128},{128,160},{160,192},{192,224},{224... | collective-permute-start | bytes 540680 | tf_op jit(solution)/shard_map/ppermute | solution.py:16
  31.5 7.0 %collective-permute-start.2 = (bf16[1,128,704]{1,2,0:T(8,128)(2,1)S(1)}, bf16[1,128,704]{1,2,0:T(8,128)(2,1)S(1)}, u32[]{:S(2)}, u32[]{:S(2)}) collective-permute-start(bf16[1,128,704]{1,2,0:T(8,128)(2,1)S(1)} %collective-permute-done.1), channel_id=1, source_target_pairs={{0,32},{32,64},{64,96},{96,128},{128,160},{160,192},{192,224},{224... | collective-permute-start | bytes 540680 | tf_op jit(solution)/shard_map/ppermute | solution.py:16
  32.0 6.6 %collective-permute-start.9 = (bf16[1,128,704]{1,2,0:T(8,128)(2,1)S(1)}, bf16[1,128,704]{1,2,0:T(8,128)(2,1)S(1)}, u32[]{:S(2)}, u32[]{:S(2)}) collective-permute-start(bf16[1,128,704]{1,2,0:T(8,128)(2,1)S(1)} %collective-permute-done.8), channel_id=1, source_target_pairs={{0,480},{32,0},{64,32},{96,64},{128,96},{160,128},{192,160},{224,1... | collective-permute-start | bytes 540680 | tf_op jit(solution)/shard_map/ppermute | solution.py:18
  38.5 7.0 %collective-permute-start.3 = (bf16[1,128,704]{1,2,0:T(8,128)(2,1)S(1)}, bf16[1,128,704]{1,2,0:T(8,128)(2,1)S(1)}, u32[]{:S(2)}, u32[]{:S(2)}) collective-permute-start(bf16[1,128,704]{1,2,0:T(8,128)(2,1)S(1)} %collective-permute-done.2), channel_id=1, source_target_pairs={{0,32},{32,64},{64,96},{96,128},{128,160},{160,192},{192,224},{224... | collective-permute-start | bytes 540680 | tf_op jit(solution)/shard_map/ppermute | solution.py:16
  38.5 7.8 %collective-permute-start.10 = (bf16[1,128,704]{1,2,0:T(8,128)(2,1)S(1)}, bf16[1,128,704]{1,2,0:T(8,128)(2,1)S(1)}, u32[]{:S(2)}, u32[]{:S(2)}) collective-permute-start(bf16[1,128,704]{1,2,0:T(8,128)(2,1)S(1)} %collective-permute-done.9), channel_id=1, source_target_pairs={{0,480},{32,0},{64,32},{96,64},{128,96},{160,128},{192,160},{224,1... | collective-permute-start | bytes 540680 | tf_op jit(solution)/shard_map/ppermute | solution.py:18
  45.5 6.8 %collective-permute-start.4 = (bf16[1,128,704]{1,2,0:T(8,128)(2,1)S(1)}, bf16[1,128,704]{1,2,0:T(8,128)(2,1)S(1)}, u32[]{:S(2)}, u32[]{:S(2)}) collective-permute-start(bf16[1,128,704]{1,2,0:T(8,128)(2,1)S(1)} %collective-permute-done.3), channel_id=1, source_target_pairs={{0,32},{32,64},{64,96},{96,128},{128,160},{160,192},{192,224},{224... | collective-permute-start | bytes 540680 | tf_op jit(solution)/shard_map/ppermute | solution.py:16
  46.3 6.7 %collective-permute-start.11 = (bf16[1,128,704]{1,2,0:T(8,128)(2,1)S(1)}, bf16[1,128,704]{1,2,0:T(8,128)(2,1)}, u32[]{:S(2)}, u32[]{:S(2)}) collective-permute-start(bf16[1,128,704]{1,2,0:T(8,128)(2,1)S(1)} %collective-permute-done.10), channel_id=1, source_target_pairs={{0,480},{32,0},{64,32},{96,64},{128,96},{160,128},{192,160},{224,1... | collective-permute-start | bytes 540680 | tf_op jit(solution)/shard_map/ppermute | solution.py:18
  52.3 6.2 %collective-permute-start.5 = (bf16[1,128,704]{1,2,0:T(8,128)(2,1)S(1)}, bf16[1,128,704]{1,2,0:T(8,128)(2,1)}, u32[]{:S(2)}, u32[]{:S(2)}) collective-permute-start(bf16[1,128,704]{1,2,0:T(8,128)(2,1)S(1)} %collective-permute-done.4), channel_id=1, source_target_pairs={{0,32},{32,64},{64,96},{96,128},{128,160},{160,192},{192,224},{224... | collective-permute-start | bytes 540680 | tf_op jit(solution)/shard_map/ppermute | solution.py:16
  53.0 149.0 %collective-permute-start.12 = (bf16[1,128,704]{1,2,0:T(8,128)(2,1)}, bf16[1,128,704]{1,2,0:T(8,128)(2,1)}, u32[]{:S(2)}, u32[]{:S(2)}) collective-permute-start(bf16[1,128,704]{1,2,0:T(8,128)(2,1)} %collective-permute-done.11), channel_id=1, source_target_pairs={{0,480},{32,0},{64,32},{96,64},{128,96},{160,128},{192,160},{224,1... | collective-permute-start | bytes 540680 | tf_op jit(solution)/shard_map/ppermute | solution.py:18
  58.5 143.6 %collective-permute-start.6 = (bf16[1,128,704]{1,2,0:T(8,128)(2,1)}, bf16[1,128,704]{1,2,0:T(8,128)(2,1)}, u32[]{:S(2)}, u32[]{:S(2)}) collective-permute-start(bf16[1,128,704]{1,2,0:T(8,128)(2,1)} %collective-permute-done.5), channel_id=1, source_target_pairs={{0,32},{32,64},{64,96},{96,128},{128,160},{160,192},{192,224},{224... | collective-permute-start | bytes 540680 | tf_op jit(solution)/shard_map/ppermute | solution.py:16
  118.7 75.3 %copy-start.27 = (f32[2048]{0:T(1024)S(1)}, f32[2048]{0:T(1024)}, u32[]{:S(2)}) copy-start(f32[2048]{0:T(1024)} %param.23) | copy-start | bytes 24580
  196.2 57.4 %all-to-all-start = ((bf16[32,16,2048]{2,1,0:T(8,128)(2,1)}), bf16[32,16,2048]{2,1,0:T(8,128)(2,1)S(1)}, u32[]{:S(2)}, u32[]{:S(2)}) async-start(bf16[32,16,2048]{2,1,0:T(8,128)(2,1)} %bitcast.20), calls=%async_computation | async-start | bytes 4194304 | tf_op jit(solution)/shard_map/all_to_all | solution.py:163
  202.0 6.5 %collective-permute-start.13 = (bf16[1,128,704]{1,2,0:T(8,128)(2,1)}, bf16[1,128,704]{1,2,0:T(8,128)(2,1)}, u32[]{:S(2)}, u32[]{:S(2)}) collective-permute-start(bf16[1,128,704]{1,2,0:T(8,128)(2,1)} %collective-permute-done.12), channel_id=1, source_target_pairs={{0,480},{32,0},{64,32},{96,64},{128,96},{160,128},{192,160},{224,1... | collective-permute-start | bytes 540680 | tf_op jit(solution)/shard_map/ppermute | solution.py:18
  202.1 11.1 %collective-permute-start.7 = (bf16[1,128,704]{1,2,0:T(8,128)(2,1)}, bf16[1,128,704]{1,2,0:T(8,128)(2,1)}, u32[]{:S(2)}, u32[]{:S(2)}) collective-permute-start(bf16[1,128,704]{1,2,0:T(8,128)(2,1)} %collective-permute-done.6), channel_id=1, source_target_pairs={{0,32},{32,64},{64,96},{96,128},{128,160},{160,192},{192,224},{224... | collective-permute-start | bytes 540680 | tf_op jit(solution)/shard_map/ppermute | solution.py:16
  208.5 27.3 %collective-permute-start.14 = (bf16[1,128,704]{1,2,0:T(8,128)(2,1)}, bf16[1,128,704]{1,2,0:T(8,128)(2,1)S(1)}, u32[]{:S(2)}, u32[]{:S(2)}) collective-permute-start(bf16[1,128,704]{1,2,0:T(8,128)(2,1)} %collective-permute-done.13), channel_id=1, source_target_pairs={{0,480},{32,0},{64,32},{96,64},{128,96},{160,128},{192,160},{224,1... | collective-permute-start | bytes 540680 | tf_op jit(solution)/shard_map/ppermute | solution.py:18
  264.4 58.5 %all-to-all-start.1 = ((bf16[32,16,2048]{2,1,0:T(8,128)(2,1)}), bf16[32,16,2048]{2,1,0:T(8,128)(2,1)S(1)}, u32[]{:S(2)}, u32[]{:S(2)}) async-start(bf16[32,16,2048]{2,1,0:T(8,128)(2,1)} %bitcast.103), calls=%async_computation.1 | async-start | bytes 4194304 | tf_op jit(solution)/shard_map/all_to_all | solution.py:177
  (24 other events, 552.7 us)
Sparse Core Ops, SparseCore 0:
  9.5 46.7 all-gather.6
  58.4 42.2 all-gather.4
  103.9 85.4 all-gather.8
  191.4 48.3 all-gather.10
